TPU v7x, 32 devices: a whole 2x2x4 slice. The times are simulated.
32 devices in a mesh: ctx: 8 (over y, x, core), dp: 4 (over z).
Axes of the slice: x: 2, y: 2, z: 4, core: 2. Of those that a mesh axis runs over, the one named last changes fastest.
Arguments:
- tokens: bfloat16 [4, 1024, 4096], P('dp', 'ctx'), may hold values from -64 to 64
- query_weight: bfloat16 [4096, 4096], P('dp', 'ctx'), may hold values from -0.09375 to 0.09375
- keyval_matrix: bfloat16 [4096, 1024], P('dp', 'ctx'), may hold values from -0.09375 to 0.09375
- grad_out: bfloat16 [4, 1024, 4096], P('dp', 'ctx'), may hold values from -6 to 6
- blocks: int32 [4, 8, 8], replicated, may hold values from 0 to 7, as said below
- counts: int32 [4, 8], replicated, may hold values from 4 to 8, as said below
Outputs:
- attended: bfloat16 [4, 1024, 4096], P('dp', 'ctx')
- grad_query_weight: float32 [4096, 4096], P('dp', 'ctx')
- grad_keyval_weight: float32 [4096, 1024], P('dp', 'ctx')
Inputs may be any that keep to these rules, and one draw needn't show every extreme that they name: For key head g and query block i, the first counts[g, i] entries of blocks[g, i] are distinct; they are the blocks i - 1, i, i + 1, 0 and 7 that exist, then random others. Entries from counts[g, i] on are block numbers that are not attended. counts[g, i] is the number of distinct blocks among i - 1, i, i + 1, 0 and 7 that exist, plus 1 to 3.
All inputs are finite; a program needn't handle non-finite values.
Results may differ from a plain program's by a relative error of at most 0.004.
The roundings to bfloat16 on the way count: a program that leaves them out, or rounds other values in their place, can miss the bound.
Values may be sent and summed in bfloat16 or wider, within the bound.
No kernel may reach another device: no remote copies, remote signals or barrier semaphores. Data moves between devices by JAX's collectives and lax.ppermute only.
A program may use at most 128 MiB of HBM per device.

v0:
```python
import jax
import jax.numpy as jnp
from jax import lax
from jax.sharding import PartitionSpec as P


def partner(block, axis, distance):
    count = lax.axis_size(axis)
    route = []
    for low in range(count):
        high = low | 1 << distance
        if high != low and high < count:
            route += [(low, high), (high, low)]
    return lax.ppermute(block, axis, route)


def attend_part(query_rows, key_rows, vals, dout, valid, scale):
    scores = (
        jnp.einsum("nqhd,nkcd->nhqkc", query_rows, key_rows, preferred_element_type=jnp.float32)
        * scale
    )
    scores = jnp.where(valid[:, None, None, :, None], scores, -jnp.inf)
    peak = jnp.max(scores, axis=(3, 4), keepdims=True)
    expo = jnp.exp(scores - peak)
    probs = expo / jnp.sum(expo, axis=(3, 4), keepdims=True)
    probs_b = probs.astype(jnp.bfloat16)
    out = jnp.einsum("nhqkc,nkcd->nqhd", probs_b, vals, preferred_element_type=jnp.float32).astype(
        jnp.bfloat16
    )
    delta = jnp.transpose(
        jnp.sum(dout.astype(jnp.float32) * out.astype(jnp.float32), axis=3), (0, 2, 1)
    )
    dprob = jnp.einsum("nqhd,nkcd->nhqkc", dout, vals, preferred_element_type=jnp.float32)
    dscore = (probs * (dprob - delta[:, :, :, None, None]) * scale).astype(jnp.bfloat16)
    dquery = jnp.einsum(
        "nhqkc,nkcd->nqhd", dscore, key_rows, preferred_element_type=jnp.float32
    ).astype(jnp.bfloat16)
    dkeys = jnp.einsum("nhqkc,nqhd->nkcd", dscore, query_rows, preferred_element_type=jnp.float32)
    dvals = jnp.einsum("nhqkc,nqhd->nkcd", probs_b, dout, preferred_element_type=jnp.float32)
    return (out, dquery, dkeys, dvals)


def attention(q_heads, keyval_rows, dout_heads, blk, cnt):
    length = q_heads.shape[0]
    head_size = keyval_rows.shape[1] // 2
    heads = q_heads.shape[1] // head_size
    nblocks, kslots = blk.shape
    block = length // nblocks
    scale = head_size ** (-0.5)
    step = 4
    groups = nblocks // step
    key_rows = keyval_rows[:, :head_size].reshape(nblocks, block, head_size)
    vals = keyval_rows[:, head_size:].reshape(nblocks, block, head_size)
    valid = lax.broadcasted_iota(jnp.int32, (nblocks, kslots), 1) < cnt[:, None]
    query_rows = q_heads.reshape(groups, step, block, heads, head_size)
    dout = dout_heads.reshape(groups, step, block, heads, head_size)

    def one_step(args):
        q_part, d_part, b_part, v_part = args
        return attend_part(q_part, key_rows[b_part], vals[b_part], d_part, v_part, scale)

    out, dquery, dkeys, dvals = lax.map(
        one_step,
        (query_rows, dout, blk.reshape(groups, step, kslots), valid.reshape(groups, step, kslots)),
    )
    dkeys = dkeys.reshape(nblocks, kslots, block, head_size)
    dvals = dvals.reshape(nblocks, kslots, block, head_size)
    onehot = (
        (blk[None, :, :] == lax.broadcasted_iota(jnp.int32, (nblocks, 1, 1), 0)) & valid[None]
    ).astype(jnp.float32)
    key_grad = jnp.einsum("bnk,nkcd->bcd", onehot, dkeys, precision=lax.Precision.HIGHEST)
    val_grad = jnp.einsum("bnk,nkcd->bcd", onehot, dvals, precision=lax.Precision.HIGHEST)
    keyval_grad = jnp.concatenate(
        [key_grad.reshape(length, head_size), val_grad.reshape(length, head_size)], axis=1
    )
    return (
        out.reshape(length, heads * head_size),
        dquery.reshape(length, heads * head_size),
        keyval_grad,
    )


def shards(tokens, query_weight, keyval_matrix, grad_out, blocks, counts):
    local_rows = tokens[0]
    group_size = lax.axis_size("ctx") // blocks.shape[0]
    group_bits = group_size.bit_length() - 1
    device = lax.axis_index("ctx")
    query_cols = query_weight.shape[1]
    query_full, keyval_part = (
        lax.all_gather(query_weight, "dp", axis=0, tiled=True),
        lax.all_gather(keyval_matrix, "dp", axis=0, tiled=True),
    )
    all_rows = lax.all_gather(local_rows, "ctx", axis=0, tiled=True)
    keyval_cols = keyval_part
    for bit in range(group_bits):
        other = partner(keyval_cols, "ctx", bit)
        upper = device >> bit & 1 == 1
        keyval_cols = jnp.where(
            upper,
            jnp.concatenate([other, keyval_cols], axis=1),
            jnp.concatenate([keyval_cols, other], axis=1),
        )
    projected = jnp.dot(
        all_rows,
        jnp.concatenate([query_full, keyval_cols], axis=1),
        preferred_element_type=jnp.float32,
    ).astype(jnp.bfloat16)
    q_heads = projected[:, :query_cols]
    keyval_rows = projected[:, query_cols:]
    dout_heads = lax.all_to_all(grad_out[0], "ctx", split_axis=1, concat_axis=0, tiled=True)
    group_index = device // group_size
    blk = lax.dynamic_index_in_dim(blocks, group_index, 0, keepdims=False)
    cnt = lax.dynamic_index_in_dim(counts, group_index, 0, keepdims=False)
    out_heads, dquery, keyval_grad = attention(q_heads, keyval_rows, dout_heads, blk, cnt)
    attended = lax.all_to_all(out_heads, "ctx", split_axis=0, concat_axis=1, tiled=True)
    summed = keyval_grad
    for bit in range(group_bits):
        summed = summed + partner(summed, "ctx", bit)
    width = summed.shape[1] // group_size
    own_grad = lax.dynamic_slice_in_dim(summed, device % group_size * width, width, 1)
    own_grad = own_grad.astype(jnp.bfloat16)
    contract = (((0,), (0,)), ((), ()))
    grad_query = lax.dot_general(all_rows, dquery, contract, preferred_element_type=jnp.float32)
    grad_keyval = lax.dot_general(all_rows, own_grad, contract, preferred_element_type=jnp.float32)
    grad_query, grad_keyval = (
        lax.psum_scatter(grad_query, "dp", scatter_dimension=0, tiled=True),
        lax.psum_scatter(grad_keyval, "dp", scatter_dimension=0, tiled=True),
    )
    return (attended[None], grad_query, grad_keyval)


def solution(mesh):
    in_specs = (
        P("dp", "ctx", None),
        P("dp", "ctx"),
        P("dp", "ctx"),
        P("dp", "ctx", None),
        P(),
        P(),
    )
    out_specs = (P("dp", "ctx", None), P("dp", "ctx"), P("dp", "ctx"))
    return jax.shard_map(shards, mesh=mesh, in_specs=in_specs, out_specs=out_specs, check_vma=False)
```

profile of v0, /device:TPU:0, one launch (start us, length us, event | category | flops | bytes accessed | tf_op | source)
XLA Modules:
  0.0 476.1 jit_solution(6639766574015722503)
XLA Ops:
  7.2 0.7 all-gather.7.cloned.1.call-update
  8.0 0.7 all-gather.5.cloned.1.call-update
  8.7 0.7 all-gather.9.cloned.1.call-update
  9.4 30.8 %all-gather.7.cloned.1.call-done = bf16[4096,128]{1,0:T(8,128)(2,1)} async-done(((bf16[1024,128]{1,0:T(8,128)(2,1)}), bf16[4096,128]{1,0:T(8,128)(2,1)}) %all-gather.7.cloned.1.call-update) | async-done | bytes 1048592 | tf_op jit(solution)/shard_map/all_gather | solution.py:91
  40.3 2.3 copy.111
  42.5 4.2 all-to-all-start
  46.9 0.7 fusion.82
  47.7 0.7 copy.76
  48.4 0.6 iota_compare_fusion.1
  49.0 3.1 maximum_select_fusion
  52.1 70.0 %all-gather.5.cloned.1.call-done = bf16[4096,512]{1,0:T(8,128)(2,1)} async-done(((bf16[1024,512]{1,0:T(8,128)(2,1)}), bf16[4096,512]{1,0:T(8,128)(2,1)}) %all-gather.5.cloned.1.call-update) | async-done | bytes 4194320 | tf_op jit(solution)/shard_map/all_gather | solution.py:90
  122.1 54.8 %all-gather.9.cloned.1.call-done = bf16[1,1024,4096]{2,1,0:T(8,128)(2,1)} async-done(((bf16[1,128,4096]{2,1,0:T(8,128)(2,1)}), bf16[1,1024,4096]{2,1,0:T(8,128)(2,1)}) %all-gather.9.cloned.1.call-update) | async-done | bytes 8388624 | tf_op jit(solution)/shard_map/all_gather | solution.py:93
  177.0 10.4 %fusion.56 = bf16[1024,768]{0,1:T(8,128)(2,1)S(1)} fusion(bf16[1,1024,4096]{2,1,0:T(8,128)(2,1)} %all-gather.9.cloned.1.call-done, bf16[4096,256]{1,0:T(8,128)(2,1)S(1)} %maximum_select_fusion, bf16[4096,512]{1,0:T(8,128)(2,1)} %all-gather.5.cloned.1.call-done), kind=kOutput, calls=%fused_computation.57 | convolution fusion | flops 6455820288 | bytes 16252928 | tf_op jit(solution)/shard_map/dot_general | solution.py:103
  187.8 1.5 reshape.109
  189.4 65.5 %while.16 = (s32[]{:T(128)}, bf16[2,4,128,4,128]{2,4,3,1,0:T(8,128)(2,1)}, bf16[2,4,128,4,128]{4,3,2,1,0:T(4,128)(2,1)}, f32[2,4,8,128,128]{4,3,2,1,0:T(8,128)},...) while((s32[]{:T(128)}, ...), condition=%wide.region_4.5_spmd, body=%wide.region_0.4_spmd.sunk | while | flops 3275222016 | bytes 218726320 | solution.py:62
  189.7 0.7 gather_fusion.1
  190.5 1.2 constant_dynamic-slice_fusion.5
  191.7 0.4 copy.131
  192.1 1.3 bitcast_reduce_fusion.2
  193.4 1.8 fusion.119
  195.2 3.4 copy-done.6
  198.6 3.2 bitcast_dynamic-update-slice_fusion.8
  201.8 2.0 copy-done.7
  203.8 0.7 gather_fusion
  204.6 6.5 %bitcast_dynamic-update-slice_fusion.6 = (bf16[2,4,128,4,128]{2,4,3,1,0:T(8,128)(2,1)}, bf16[4,128,4,128]{3,1,2,0:T(8,128)(2,1)S(1)}) fusion(bf16[2,4,128,4,128]{2,4,3,1,0:T(8,128)(2,1)} %get-tuple-element.241, s32[]{:T(128)} %get-tuple-element.240, bf16[4,8,128,128,1]{3,2,4,1,0:T(8,128)(2,1)S(1)} %bitcast.231, f32[4,4,128]{2,1,0:T(4,128)S(1)} %fusion.119, ...), kind=kOutput, calls=%fused_computation.26.clone.1 | convolution fusion | flops 547618816 | bytes 10502688 | tf_op jit(solution)/shard_map/while/body/eval_jaxpr/nhqkc,nkcd->nqhd/dot_general | solution.py:27
  211.1 1.2 multiply_reduce_fusion.2
  212.3 4.3 fusion.120
  216.7 1.3 bitcast_dynamic-update-slice_fusion.7
  218.0 1.9 copy-done.5
  219.9 0.8 fusion.121
  220.7 0.3 copy.132
  221.3 1.0 copy-done.10
  222.4 0.7 gather_fusion.1
  223.1 1.2 constant_dynamic-slice_fusion.5
  224.4 0.4 copy.131
  224.7 1.3 bitcast_reduce_fusion.2
  226.0 1.8 fusion.119
  227.9 3.4 copy-done.6
  231.2 3.2 bitcast_dynamic-update-slice_fusion.8
  234.5 2.0 copy-done.7
  236.4 0.7 gather_fusion
  237.2 6.5 %bitcast_dynamic-update-slice_fusion.6 = (bf16[2,4,128,4,128]{2,4,3,1,0:T(8,128)(2,1)}, bf16[4,128,4,128]{3,1,2,0:T(8,128)(2,1)S(1)}) fusion(bf16[2,4,128,4,128]{2,4,3,1,0:T(8,128)(2,1)} %get-tuple-element.241, s32[]{:T(128)} %get-tuple-element.240, bf16[4,8,128,128,1]{3,2,4,1,0:T(8,128)(2,1)S(1)} %bitcast.231, f32[4,4,128]{2,1,0:T(4,128)S(1)} %fusion.119, ...), kind=kOutput, calls=%fused_computation.26.clone.1 | convolution fusion | flops 547618816 | bytes 10502688 | tf_op jit(solution)/shard_map/while/body/eval_jaxpr/nhqkc,nkcd->nqhd/dot_general | solution.py:27
  243.7 1.2 multiply_reduce_fusion.2
  245.0 4.3 fusion.120
  249.3 1.3 bitcast_dynamic-update-slice_fusion.7
  250.6 1.9 copy-done.5
  252.5 0.8 fusion.121
  253.4 0.3 copy.132
  253.9 1.0 copy-done.10
  254.9 7.2 %fusion.61 = f32[8,128,128]{2,0,1:T(8,128)S(1)} fusion(f32[8,8,128,128]{3,2,1,0:T(8,128)} %bitcast.237, s32[8,8]{0,1:T(8,128)S(1)} %copy-done.13, pred[8,8]{0,1:T(8,128)(4,1)S(1)} %copy-done.14), kind=kOutput, calls=%fused_computation.61 | convolution fusion | flops 100664320 | bytes 4718912 | tf_op jit(solution)/shard_map/bnk,nkcd->bcd/dot_general | solution.py:71
  262.3 5.0 %fusion.64 = f32[8,128,128]{2,0,1:T(8,128)S(1)} fusion(f32[8,8,128,128]{3,2,1,0:T(8,128)S(1)} %bitcast.238, s32[8,8]{0,1:T(8,128)S(1)} %copy-done.13, pred[8,8]{0,1:T(8,128)(4,1)S(1)} %copy-done.14), kind=kOutput, calls=%fused_computation.62 | convolution fusion | flops 100664320 | bytes 4718912 | tf_op jit(solution)/shard_map/bnk,nkcd->bcd/dot_general | solution.py:72
  267.5 0.3 collective-permute-start.1
  267.8 2.5 collective-permute-done.1
  270.3 6.2 %fusion.44 = f32[4096,128]{0,1:T(8,128)} fusion(bf16[1,1024,4096]{2,1,0:T(8,128)(2,1)} %all-gather.9.cloned.1.call-done, s32[]{:T(128)S(6)} %select_n.51, f32[1024,128]{1,0:T(8,128)S(1)} %bitcast.234, f32[1024,128]{1,0:T(8,128)S(1)} %bitcast.236, f32[1024,256]{1,0:T(8,128)} %collective-permute-done.1), kind=kOutput, calls=%fused_computation.50 | convolution fusion | flops 1074135040 | bytes 12058628 | tf_op jit(solution)/shard_map/dot_general | solution.py:124
  276.6 10.4 %fusion.38 = f32[4096,512]{0,1:T(8,128)} fusion(bf16[1,1024,4096]{2,1,0:T(8,128)(2,1)} %all-gather.9.cloned.1.call-done, bf16[128,8,4,128]{3,2,1,0:T(4,128)(2,1)S(1)} %bitcast.240), kind=kOutput, calls=%fused_computation.46 | convolution fusion | flops 4294967296 | bytes 17825792 | tf_op jit(solution)/shard_map/dot_general | solution.py:123
  287.0 1.2 copy-done.12
  288.2 0.5 copy.112
  288.7 17.9 %all_to_all.32 = bf16[8,128,512]{2,1,0:T(8,128)(2,1)S(1)} all-to-all(bf16[8,128,512]{2,1,0:T(8,128)(2,1)S(1)} %copy.112), channel_id=1, replica_groups=mesh['ctx'=8,'dp'=4] {'ctx'}, dimensions={0} | all-to-all | bytes 2097152 | tf_op jit(solution)/shard_map/all_to_all | solution.py:115
  306.6 0.7 copy.74
  307.3 1.3 copy.81
  308.6 11.9 %reduce-scatter.5.cloned.1.call-done = f32[1024,128]{0,1:T(8,128)} async-done(((f32[4096,128]{0,1:T(8,128)}), f32[1024,128]{0,1:T(8,128)}) %reduce-scatter.5.cloned.1.call-update) | async-done | bytes 524304 | tf_op jit(solution)/shard_map/reduce_scatter | solution.py:127
  320.5 2.0 copy.83
  322.6 144.1 %reduce-scatter.3.cloned.1.call-done = f32[1024,512]{0,1:T(8,128)} async-done(((f32[4096,512]{0,1:T(8,128)}), f32[1024,512]{0,1:T(8,128)}) %reduce-scatter.3.cloned.1.call-update) | async-done | bytes 2097168 | tf_op jit(solution)/shard_map/reduce_scatter | solution.py:126
  466.7 2.9 copy.82
  (72 shorter events, 1.9 us)
Async XLA Ops:
  7.2 40.5 %copy-start = (s32[4,8,8]{2,1,0:T(8,128)S(1)}, s32[4,8,8]{2,1,0:T(8,128)}, u32[]{:S(2)}) copy-start(s32[4,8,8]{2,1,0:T(8,128)} %param.12) | copy-start | bytes 3076
  7.2 33.1 %all-gather.7.cloned.1.call-start = ((), (), s32[]{:S(2)}) async-start(), calls=%async_computation.5 | async-start | bytes 1310720 | tf_op jit(solution)/shard_map/all_gather | solution.py:91
  7.9 114.2 %all-gather.5.cloned.1.call-start = ((), (), s32[]{:S(2)}) async-start(), calls=%async_computation.4 | async-start | bytes 5242880 | tf_op jit(solution)/shard_map/all_gather | solution.py:90
  8.7 168.3 %all-gather.9.cloned.1.call-start = ((), (), s32[]{:S(2)}) async-start(), calls=%async_computation.8 | async-start | bytes 9437184 | tf_op jit(solution)/shard_map/all_gather | solution.py:93
  40.2 8.8 %collective-permute-start = (bf16[4096,128]{1,0:T(8,128)(2,1)}, bf16[4096,128]{1,0:T(8,128)(2,1)}, u32[]{:S(2)}, u32[]{:S(2)}) collective-permute-start(bf16[4096,128]{1,0:T(8,128)(2,1)} %all-gather.7.cloned.1.call-done), channel_id=1, source_target_pairs={{0,4},{4,0},{8,12},{12,8},{16,20},{20,16},{24,28},{28,24},{1,5},{5... | collective-permute-start | bytes 3145736 | tf_op jit(solution)/shard_map/ppermute | solution.py:14
  42.5 146.9 %all-to-all-start = ((bf16[128,8,512]{0,2,1:T(8,128)(2,1)}), bf16[128,8,512]{0,2,1:T(8,128)(2,1)}, u32[]{:S(2)}, u32[]{:S(2)}) async-start(bf16[128,8,512]{0,2,1:T(8,128)(2,1)} %bitcast.39), calls=%async_computation | async-start | bytes 2097152 | tf_op jit(solution)/shard_map/all_to_all | solution.py:110
  46.8 273.8 %reduce-scatter.5.cloned.1.call-start = ((), (), s32[]{:S(2)}) async-start(), calls=%async_computation.7 | async-start | bytes 2621440 | tf_op jit(solution)/shard_map/reduce_scatter | solution.py:127
  189.4 65.5 %copy-start.13 = (s32[8,8]{0,1:T(8,128)S(1)}, s32[8,8]{0,1:T(8,128)}, u32[]{:S(2)}) copy-start(s32[8,8]{0,1:T(8,128)} %copy.76) | copy-start | bytes 772
  189.4 65.5 %copy-start.14 = (pred[8,8]{0,1:T(8,128)(4,1)S(1)}, pred[8,8]{0,1:T(8,128)(4,1)}, u32[]{:S(2)}) copy-start(pred[8,8]{0,1:T(8,128)(4,1)} %iota_compare_fusion.1) | copy-start | bytes 196
  193.4 8.4 %copy-start.2 = (f32[4,8,128,128,4]{3,2,4,1,0:T(8,128)}, f32[4,8,128,128,4]{3,2,4,1,0:T(8,128)S(1)}, u32[]{:S(2)}) copy-start(f32[4,8,128,128,4]{3,2,4,1,0:T(8,128)S(1)} %get-tuple-element.224) | copy-start | bytes 25165828 | tf_op jit(solution)/shard_map/while
  193.4 5.2 %copy-start.6 = (f32[2,4,8,128,128]{4,3,2,1,0:T(8,128)S(1)}, f32[2,4,8,128,128]{4,3,2,1,0:T(8,128)}, u32[]{:S(2)}) copy-start(f32[2,4,8,128,128]{4,3,2,1,0:T(8,128)} %get-tuple-element.244) | copy-start | bytes 12582916 | tf_op jit(solution)/shard_map/while
  201.8 2.0 copy-start.7
  204.5 7.8 %copy-start.3 = (f32[4,8,128,128,4]{3,2,4,1,0:T(8,128)S(1)}, f32[4,8,128,128,4]{3,2,4,1,0:T(8,128)}, u32[]{:S(2)}) copy-start(f32[4,8,128,128,4]{3,2,4,1,0:T(8,128)} %copy-done.2) | copy-start | bytes 25165828 | tf_op jit(solution)/shard_map/while
  212.3 4.4 copy-start.4
  216.7 4.4 copy-start.9
  218.0 1.9 copy-start.5
  221.3 1.0 copy-start.10
  226.0 8.4 %copy-start.2 = (f32[4,8,128,128,4]{3,2,4,1,0:T(8,128)}, f32[4,8,128,128,4]{3,2,4,1,0:T(8,128)S(1)}, u32[]{:S(2)}) copy-start(f32[4,8,128,128,4]{3,2,4,1,0:T(8,128)S(1)} %get-tuple-element.224) | copy-start | bytes 25165828 | tf_op jit(solution)/shard_map/while
  226.0 5.2 %copy-start.6 = (f32[2,4,8,128,128]{4,3,2,1,0:T(8,128)S(1)}, f32[2,4,8,128,128]{4,3,2,1,0:T(8,128)}, u32[]{:S(2)}) copy-start(f32[2,4,8,128,128]{4,3,2,1,0:T(8,128)} %get-tuple-element.244) | copy-start | bytes 12582916 | tf_op jit(solution)/shard_map/while
  234.4 2.0 copy-start.7
  237.2 7.8 %copy-start.3 = (f32[4,8,128,128,4]{3,2,4,1,0:T(8,128)S(1)}, f32[4,8,128,128,4]{3,2,4,1,0:T(8,128)}, u32[]{:S(2)}) copy-start(f32[4,8,128,128,4]{3,2,4,1,0:T(8,128)} %copy-done.2) | copy-start | bytes 25165828 | tf_op jit(solution)/shard_map/while
  245.0 4.4 copy-start.4
  249.3 4.4 copy-start.9
  250.6 1.9 copy-start.5
  253.9 1.0 copy-start.10
  254.9 7.4 %copy-start.8 = (f32[2,4,8,128,128]{4,3,2,1,0:T(8,128)S(1)}, f32[2,4,8,128,128]{4,3,2,1,0:T(8,128)}, u32[]{:S(2)}) copy-start(f32[2,4,8,128,128]{4,3,2,1,0:T(8,128)} %get-tuple-element.66) | copy-start | bytes 12582916
  267.5 2.9 collective-permute-start.1
  267.8 8.8 %copy-start.11 = (bf16[2,4,128,4,128]{4,3,2,1,0:T(4,128)(2,1)S(1)}, bf16[2,4,128,4,128]{4,3,2,1,0:T(4,128)(2,1)}, u32[]{:S(2)}) copy-start(bf16[2,4,128,4,128]{4,3,2,1,0:T(4,128)(2,1)} %get-tuple-element.64) | copy-start | bytes 3145732
  276.5 190.2 %reduce-scatter.3.cloned.1.call-start = ((), (), s32[]{:S(2)}) async-start(), calls=%async_computation.6 | async-start | bytes 10485760 | tf_op jit(solution)/shard_map/reduce_scatter | solution.py:126
  287.0 1.2 copy-start.12
  288.2 181.4 %copy-start.1 = (s32[4,8,8]{2,1,0:T(8,128)S(1)}, s32[4,8,8]{2,1,0:T(8,128)}, u32[]{:S(2)}) copy-start(s32[4,8,8]{2,1,0:T(8,128)} %param.12) | copy-start | bytes 3076
Sparse Core Ops, SparseCore 0:
  9.6 30.6 all-gather.6
  41.8 80.2 all-gather.4
  124.0 52.9 all-gather.8
  276.6 43.8 reduce-scatter.4
  322.9 143.8 reduce-scatter.2
where the time goes:
time: 477 us; the launch traced here: 476 us
  waiting for transfers between devices  316 us (66%)
  matrix products  74 us (16%)
  local copies, waits for them, and re-layouts  38.6 us (8%)
  blocking collectives  17.9 us (4%)
  between operations  14 us (3%)
  other arithmetic  9.91 us (2%)
    reduce_scatter x1, waiting for transfers between devices, shards(): lax.psum_scatter(grad_query, 'dp', scatter_dimension=0, tiled=True)  144 us
    all_gather x1, waiting for transfers between devices, shards(): lax.all_gather(query_weight, 'dp', axis=0, tiled=True)  70 us
    all_gather x1, waiting for transfers between devices, shards(): all_rows = lax.all_gather(local_rows, 'ctx', axis=0, tiled=True)  54.8 us
    all_gather x1, waiting for transfers between devices, shards(): lax.all_gather(keyval_matrix, 'dp', axis=0, tiled=True)  30.8 us
    all_to_all x1, blocking collectives, shards(): lax.all_to_all(out_heads, 'ctx', split_axis=0, concat_axis=1, tiled=True)  17.9 us
    while x32, local copies, waits for them, and re-layouts  16.6 us
    dot_general x2, matrix products, attend_part(): jnp.einsum('nhqkc,nkcd->nqhd', probs_b, vals, preferred_element_type=jnp....  13.1 us
    reduce_scatter x1, waiting for transfers between devices, shards(): lax.psum_scatter(grad_keyval, 'dp', scatter_dimension=0, tiled=True)  11.9 us
  transfers between devices with their start and end apart: 8, of which 6 were waited for; matrix products, arithmetic and copies ran while one was open for 7% of the time, Pallas kernels for 0%

commit v1 on v0

--- a/solution.py
+++ b/solution.py
@@ -2,6 +2,22 @@
 import jax.numpy as jnp
 from jax import lax
 from jax.sharding import PartitionSpec as P
+
+
+def ring_gather(x, axis, dim):
+    ways, here, step = (lax.axis_size(axis), lax.axis_index(axis), x.shape[dim])
+    shape = [n * ways if d == dim else n for d, n in enumerate(x.shape)]
+    full = lax.dynamic_update_slice_in_dim(jnp.zeros(shape, x.dtype), x, here * step, axis=dim)
+    going_up = going_down = x
+    for far in range(1, ways // 2 + 1):
+        going_up = lax.ppermute(going_up, axis, [(d, (d + 1) % ways) for d in range(ways)])
+        full = lax.dynamic_update_slice_in_dim(full, going_up, (here - far) % ways * step, axis=dim)
+        if 2 * far < ways:
+            going_down = lax.ppermute(going_down, axis, [(d, (d - 1) % ways) for d in range(ways)])
+            full = lax.dynamic_update_slice_in_dim(
+                full, going_down, (here + far) % ways * step, axis=dim
+            )
+    return full
 
 
 def partner(block, axis, distance):
@@ -88,7 +104,7 @@
     query_cols = query_weight.shape[1]
     query_full, keyval_part = (
         lax.all_gather(query_weight, "dp", axis=0, tiled=True),
-        lax.all_gather(keyval_matrix, "dp", axis=0, tiled=True),
+        ring_gather(keyval_matrix, "dp", 0),
     )
     all_rows = lax.all_gather(local_rows, "ctx", axis=0, tiled=True)
     keyval_cols = keyval_part

time: 477 us -> 457 us (0.958)
  waiting for transfers between devices: 316 us -> 289 us
  starting transfers between devices: 4.76 us -> 9.99 us
    all_gather x1 -> x0, waiting for transfers between devices: 30.8 us -> none  [shards(): lax.all_gather(keyval_matrix, 'dp', axis=0, tiled=True)]
    ppermute x0 -> x3, waiting for transfers between devices: none -> 23.5 us  [the longest x2 15.7 us: ring_gather(): lax.ppermute(going_up, axis, [(d, (d + 1) % ways) for d in range(ways)])]
    all_gather x1, waiting for transfers between devices: 70 us -> 50 us  [shards(): lax.all_gather(query_weight, 'dp', axis=0, tiled=True)]
    ppermute x0 -> x3, starting transfers between devices: none -> 5.17 us  [the longest x2 3.08 us: ring_gather(): lax.ppermute(going_up, axis, [(d, (d + 1) % ways) for d in range(ways)])]
  transfers between devices with their start and end apart: 8 -> 10, of which waited for: 6 -> 8; matrix products, arithmetic and copies ran while one was open for 7% -> 8% of each run, Pallas kernels for 0% -> 0%
where the time goes in v1:
time: 457 us
  waiting for transfers between devices  289 us (63%)
  matrix products  74.1 us (16%)
  local copies, waits for them, and re-layouts  42.1 us (9%)
  blocking collectives  17.9 us (4%)
  between operations  14.1 us (3%)
  starting transfers between devices  9.99 us (2%)
  other arithmetic  8.97 us (2%)
    reduce_scatter x1, waiting for transfers between devices, shards(): lax.psum_scatter(grad_query, 'dp', scatter_dimension=0, tiled=True)  144 us
    all_gather x1, waiting for transfers between devices, shards(): all_rows = lax.all_gather(local_rows, 'ctx', axis=0, tiled=True)  55.5 us
    all_gather x1, waiting for transfers between devices, shards(): lax.all_gather(query_weight, 'dp', axis=0, tiled=True)  50 us
    all_to_all x1, blocking collectives, shards(): lax.all_to_all(out_heads, 'ctx', split_axis=0, concat_axis=1, tiled=True)  17.9 us
    while x32, local copies, waits for them, and re-layouts  16.5 us
    ppermute x2, waiting for transfers between devices, ring_gather(): lax.ppermute(going_up, axis, [(d, (d + 1) % ways) for d in range(ways)])  15.7 us
    dot_general x2, matrix products, attend_part(): jnp.einsum('nhqkc,nkcd->nqhd', probs_b, vals, preferred_element_type=jnp....  13.1 us
    reduce_scatter x1, waiting for transfers between devices, shards(): lax.psum_scatter(grad_keyval, 'dp', scatter_dimension=0, tiled=True)  11.8 us
  transfers between devices with their start and end apart: 10, of which 8 were waited for; matrix products, arithmetic and copies ran while one was open for 8% of the time, Pallas kernels for 0%

profile of v1, /device:TPU:0, one launch (start us, length us, event | category | flops | bytes accessed | tf_op | source)
XLA Modules:
  0.0 456.7 jit_solution(9961825338445962620)
XLA Ops:
  7.2 0.7 all-gather.4.cloned.1.call-update
  8.0 0.7 all-gather.6.cloned.1.call-update
  8.7 3.1 collective-permute-start
  11.7 2.1 collective-permute-start.1
  13.8 7.3 %collective-permute-done = bf16[1024,128]{1,0:T(8,128)(2,1)S(1)} collective-permute-done((bf16[1024,128]{1,0:T(8,128)(2,1)}, bf16[1024,128]{1,0:T(8,128)(2,1)S(1)}, u32[]{:S(2)}, u32[]{:S(2)}) %collective-permute-start) | collective-permute-done | bytes 262176 | tf_op jit(solution)/shard_map/ppermute | solution.py:13
  21.3 1.0 constant_dynamic-update-slice_fusion.4
  22.4 7.9 %collective-permute-done.1 = bf16[1024,128]{1,0:T(8,128)(2,1)S(1)} collective-permute-done((bf16[1024,128]{1,0:T(8,128)(2,1)}, bf16[1024,128]{1,0:T(8,128)(2,1)S(1)}, u32[]{:S(2)}, u32[]{:S(2)}) %collective-permute-start.1) | collective-permute-done | bytes 262176 | tf_op jit(solution)/shard_map/ppermute | solution.py:16
  30.3 8.4 %collective-permute-done.2 = bf16[1024,128]{1,0:T(8,128)(2,1)S(1)} collective-permute-done((bf16[1024,128]{1,0:T(8,128)(2,1)S(1)}, bf16[1024,128]{1,0:T(8,128)(2,1)S(1)}, u32[]{:S(2)}, u32[]{:S(2)}) %collective-permute-start.2) | collective-permute-done | bytes 262176 | tf_op jit(solution)/shard_map/ppermute | solution.py:13
  38.8 2.3 copy.111
  41.1 4.2 all-to-all-start
  45.5 0.7 fusion.82
  46.2 0.7 copy.76
  46.9 0.5 iota_compare_fusion.1
  47.5 2.2 maximum_select_fusion
  49.7 50.0 %all-gather.4.cloned.1.call-done = bf16[4096,512]{1,0:T(8,128)(2,1)} async-done(((bf16[1024,512]{1,0:T(8,128)(2,1)}), bf16[4096,512]{1,0:T(8,128)(2,1)}) %all-gather.4.cloned.1.call-update) | async-done | bytes 4194320 | tf_op jit(solution)/shard_map/all_gather | solution.py:106
  99.8 55.5 %all-gather.6.cloned.1.call-done = bf16[1,1024,4096]{2,1,0:T(8,128)(2,1)} async-done(((bf16[1,128,4096]{2,1,0:T(8,128)(2,1)}), bf16[1,1024,4096]{2,1,0:T(8,128)(2,1)}) %all-gather.6.cloned.1.call-update) | async-done | bytes 8388624 | tf_op jit(solution)/shard_map/all_gather | solution.py:109
  155.2 10.4 %fusion.56 = bf16[1024,768]{0,1:T(8,128)(2,1)S(1)} fusion(bf16[1,1024,4096]{2,1,0:T(8,128)(2,1)} %all-gather.6.cloned.1.call-done, bf16[4096,256]{1,0:T(8,128)(2,1)S(1)} %maximum_select_fusion, bf16[4096,512]{1,0:T(8,128)(2,1)} %all-gather.4.cloned.1.call-done), kind=kOutput, calls=%fused_computation.57 | convolution fusion | flops 6455820288 | bytes 16252928 | tf_op jit(solution)/shard_map/dot_general | solution.py:119
  165.7 1.1 copy-done.9
  166.9 1.6 reshape.109
  168.5 1.1 fusion.86
  169.9 65.5 %while.16 = (s32[]{:T(128)}, bf16[2,4,128,4,128]{2,4,3,1,0:T(8,128)(2,1)}, bf16[2,4,128,4,128]{4,3,2,1,0:T(4,128)(2,1)}, f32[2,4,8,128,128]{4,3,2,1,0:T(8,128)},...) while((s32[]{:T(128)}, ...), condition=%wide.region_4.5_spmd, body=%wide.region_0.4_spmd.sunk | while | flops 3275222016 | bytes 218726320 | solution.py:78
  170.2 0.7 gather_fusion.1
  171.0 1.2 constant_dynamic-slice_fusion.5
  172.6 1.3 bitcast_reduce_fusion.2
  173.9 1.8 fusion.119
  175.7 3.4 copy-done.6
  179.1 3.2 bitcast_dynamic-update-slice_fusion.8
  182.3 2.0 copy-done.7
  184.3 0.7 gather_fusion
  185.1 6.5 %bitcast_dynamic-update-slice_fusion.6 = (bf16[2,4,128,4,128]{2,4,3,1,0:T(8,128)(2,1)}, bf16[4,128,4,128]{3,1,2,0:T(8,128)(2,1)S(1)}) fusion(bf16[2,4,128,4,128]{2,4,3,1,0:T(8,128)(2,1)} %get-tuple-element.241, s32[]{:T(128)} %get-tuple-element.240, bf16[4,8,128,128,1]{3,2,4,1,0:T(8,128)(2,1)S(1)} %bitcast.231, f32[4,4,128]{2,1,0:T(4,128)S(1)} %fusion.119, ...), kind=kOutput, calls=%fused_computation.26.clone.1 | convolution fusion | flops 547618816 | bytes 10502688 | tf_op jit(solution)/shard_map/while/body/eval_jaxpr/nhqkc,nkcd->nqhd/dot_general | solution.py:43
  191.6 1.2 multiply_reduce_fusion.2
  192.8 4.3 fusion.120
  197.2 1.3 bitcast_dynamic-update-slice_fusion.7
  198.5 1.9 copy-done.5
  200.4 0.8 fusion.121
  201.8 1.0 copy-done.11
  202.9 0.7 gather_fusion.1
  203.6 1.2 constant_dynamic-slice_fusion.5
  205.2 1.3 bitcast_reduce_fusion.2
  206.5 1.8 fusion.119
  208.4 3.4 copy-done.6
  211.8 3.2 bitcast_dynamic-update-slice_fusion.8
  215.0 2.0 copy-done.7
  217.0 0.7 gather_fusion
  217.7 6.5 %bitcast_dynamic-update-slice_fusion.6 = (bf16[2,4,128,4,128]{2,4,3,1,0:T(8,128)(2,1)}, bf16[4,128,4,128]{3,1,2,0:T(8,128)(2,1)S(1)}) fusion(bf16[2,4,128,4,128]{2,4,3,1,0:T(8,128)(2,1)} %get-tuple-element.241, s32[]{:T(128)} %get-tuple-element.240, bf16[4,8,128,128,1]{3,2,4,1,0:T(8,128)(2,1)S(1)} %bitcast.231, f32[4,4,128]{2,1,0:T(4,128)S(1)} %fusion.119, ...), kind=kOutput, calls=%fused_computation.26.clone.1 | convolution fusion | flops 547618816 | bytes 10502688 | tf_op jit(solution)/shard_map/while/body/eval_jaxpr/nhqkc,nkcd->nqhd/dot_general | solution.py:43
  224.3 1.2 multiply_reduce_fusion.2
  225.5 4.3 fusion.120
  229.9 1.3 bitcast_dynamic-update-slice_fusion.7
  231.1 1.9 copy-done.5
  233.1 0.8 fusion.121
  234.5 1.0 copy-done.11
  235.4 7.2 %fusion.61 = f32[8,128,128]{2,0,1:T(8,128)S(1)} fusion(f32[8,8,128,128]{3,2,1,0:T(8,128)} %bitcast.237, s32[8,8]{0,1:T(8,128)S(1)} %copy-done.14, pred[8,8]{0,1:T(8,128)(4,1)S(1)} %copy-done.15), kind=kOutput, calls=%fused_computation.61 | convolution fusion | flops 100664320 | bytes 4718912 | tf_op jit(solution)/shard_map/bnk,nkcd->bcd/dot_general | solution.py:87
  242.8 5.0 %fusion.64 = f32[8,128,128]{2,0,1:T(8,128)S(1)} fusion(f32[8,8,128,128]{3,2,1,0:T(8,128)S(1)} %bitcast.238, s32[8,8]{0,1:T(8,128)S(1)} %copy-done.14, pred[8,8]{0,1:T(8,128)(4,1)S(1)} %copy-done.15), kind=kOutput, calls=%fused_computation.62 | convolution fusion | flops 100664320 | bytes 4718912 | tf_op jit(solution)/shard_map/bnk,nkcd->bcd/dot_general | solution.py:88
  248.3 2.5 collective-permute-done.4
  250.8 6.2 %fusion.44 = f32[4096,128]{0,1:T(8,128)} fusion(bf16[1,1024,4096]{2,1,0:T(8,128)(2,1)} %all-gather.6.cloned.1.call-done, s32[]{:T(128)S(6)} %select_n.82, f32[1024,128]{1,0:T(8,128)S(1)} %bitcast.234, f32[1024,128]{1,0:T(8,128)S(1)} %bitcast.236, f32[1024,256]{1,0:T(8,128)} %collective-permute-done.4), kind=kOutput, calls=%fused_computation.50 | convolution fusion | flops 1074135040 | bytes 12058628 | tf_op jit(solution)/shard_map/dot_general | solution.py:140
  257.1 10.4 %fusion.38 = f32[4096,512]{0,1:T(8,128)} fusion(bf16[1,1024,4096]{2,1,0:T(8,128)(2,1)} %all-gather.6.cloned.1.call-done, bf16[128,8,4,128]{3,2,1,0:T(4,128)(2,1)S(1)} %bitcast.240), kind=kOutput, calls=%fused_computation.46 | convolution fusion | flops 4294967296 | bytes 17825792 | tf_op jit(solution)/shard_map/dot_general | solution.py:139
  267.5 1.2 copy-done.13
  269.3 17.9 %all_to_all.32 = bf16[8,128,512]{2,1,0:T(8,128)(2,1)S(1)} all-to-all(bf16[8,128,512]{2,1,0:T(8,128)(2,1)S(1)} %copy.112), channel_id=1, replica_groups=mesh['ctx'=8,'dp'=4] {'ctx'}, dimensions={0} | all-to-all | bytes 2097152 | tf_op jit(solution)/shard_map/all_to_all | solution.py:131
  287.2 0.7 copy.74
  287.8 1.3 copy.81
  289.2 11.8 %reduce-scatter.5.cloned.1.call-done = f32[1024,128]{0,1:T(8,128)} async-done(((f32[4096,128]{0,1:T(8,128)}), f32[1024,128]{0,1:T(8,128)}) %reduce-scatter.5.cloned.1.call-update) | async-done | bytes 524304 | tf_op jit(solution)/shard_map/reduce_scatter | solution.py:143
  301.0 2.0 copy.83
  303.0 144.2 %reduce-scatter.3.cloned.1.call-done = f32[1024,512]{0,1:T(8,128)} async-done(((f32[4096,512]{0,1:T(8,128)}), f32[1024,512]{0,1:T(8,128)}) %reduce-scatter.3.cloned.1.call-update) | async-done | bytes 2097168 | tf_op jit(solution)/shard_map/reduce_scatter | solution.py:142
  447.2 2.9 copy.82
  (82 shorter events, 4.4 us)
Async XLA Ops:
  7.2 39.1 %copy-start = (s32[4,8,8]{2,1,0:T(8,128)S(1)}, s32[4,8,8]{2,1,0:T(8,128)}, u32[]{:S(2)}) copy-start(s32[4,8,8]{2,1,0:T(8,128)} %param.12) | copy-start | bytes 3076
  7.2 92.6 %all-gather.4.cloned.1.call-start = ((), (), s32[]{:S(2)}) async-start(), calls=%async_computation.4 | async-start | bytes 5242880 | tf_op jit(solution)/shard_map/all_gather | solution.py:106
  7.9 147.3 %all-gather.6.cloned.1.call-start = ((), (), s32[]{:S(2)}) async-start(), calls=%async_computation.7 | async-start | bytes 9437184 | tf_op jit(solution)/shard_map/all_gather | solution.py:109
  8.7 12.5 %collective-permute-start = (bf16[1024,128]{1,0:T(8,128)(2,1)}, bf16[1024,128]{1,0:T(8,128)(2,1)S(1)}, u32[]{:S(2)}, u32[]{:S(2)}) collective-permute-start(bf16[1024,128]{1,0:T(8,128)(2,1)} %param.10), channel_id=1, source_target_pairs={{0,1},{1,2},{2,3},{3,0},{4,5},{5,6},{6,7},{7,4},{8,9},{9,10},{10,1... | collective-permute-start | bytes 786440 | tf_op jit(solution)/shard_map/ppermute | solution.py:13
  11.7 18.5 %collective-permute-start.1 = (bf16[1024,128]{1,0:T(8,128)(2,1)}, bf16[1024,128]{1,0:T(8,128)(2,1)S(1)}, u32[]{:S(2)}, u32[]{:S(2)}) collective-permute-start(bf16[1024,128]{1,0:T(8,128)(2,1)} %param.10), channel_id=1, source_target_pairs={{0,3},{1,0},{2,1},{3,2},{4,7},{5,4},{6,5},{7,6},{8,11},{9,8},{10,9... | collective-permute-start | bytes 786440 | tf_op jit(solution)/shard_map/ppermute | solution.py:16
  21.2 17.5 %collective-permute-start.2 = (bf16[1024,128]{1,0:T(8,128)(2,1)S(1)}, bf16[1024,128]{1,0:T(8,128)(2,1)S(1)}, u32[]{:S(2)}, u32[]{:S(2)}) collective-permute-start(bf16[1024,128]{1,0:T(8,128)(2,1)S(1)} %collective-permute-done), channel_id=1, source_target_pairs={{0,1},{1,2},{2,3},{3,0},{4,5},{5,6},{6,7},{7,4},{8,9},{9,10},{10,1... | collective-permute-start | bytes 786440 | tf_op jit(solution)/shard_map/ppermute | solution.py:13
  38.7 8.8 %collective-permute-start.3 = (bf16[4096,128]{1,0:T(8,128)(2,1)S(1)}, bf16[4096,128]{1,0:T(8,128)(2,1)}, u32[]{:S(2)}, u32[]{:S(2)}) collective-permute-start(bf16[4096,128]{1,0:T(8,128)(2,1)S(1)} %constant_dynamic-update-slice_fusion.1), channel_id=1, source_target_pairs={{0,4},{4,0},{8,12},{12,8},{16,20},{20,16},{24,28},{28,24},{1,5},{5... | collective-permute-start | bytes 3145736 | tf_op jit(solution)/shard_map/ppermute | solution.py:30
  41.1 128.8 %all-to-all-start = ((bf16[128,8,512]{0,2,1:T(8,128)(2,1)}), bf16[128,8,512]{0,2,1:T(8,128)(2,1)}, u32[]{:S(2)}, u32[]{:S(2)}) async-start(bf16[128,8,512]{0,2,1:T(8,128)(2,1)} %bitcast.39), calls=%async_computation | async-start | bytes 2097152 | tf_op jit(solution)/shard_map/all_to_all | solution.py:126
  45.3 255.7 %reduce-scatter.5.cloned.1.call-start = ((), (), s32[]{:S(2)}) async-start(), calls=%async_computation.6 | async-start | bytes 2621440 | tf_op jit(solution)/shard_map/reduce_scatter | solution.py:143
  165.7 1.1 copy-start.9
  169.9 65.5 %copy-start.14 = (s32[8,8]{0,1:T(8,128)S(1)}, s32[8,8]{0,1:T(8,128)}, u32[]{:S(2)}) copy-start(s32[8,8]{0,1:T(8,128)} %copy.76) | copy-start | bytes 772
  169.9 65.5 %copy-start.15 = (pred[8,8]{0,1:T(8,128)(4,1)S(1)}, pred[8,8]{0,1:T(8,128)(4,1)}, u32[]{:S(2)}) copy-start(pred[8,8]{0,1:T(8,128)(4,1)} %iota_compare_fusion.1) | copy-start | bytes 196
  173.9 8.4 %copy-start.2 = (f32[4,8,128,128,4]{3,2,4,1,0:T(8,128)}, f32[4,8,128,128,4]{3,2,4,1,0:T(8,128)S(1)}, u32[]{:S(2)}) copy-start(f32[4,8,128,128,4]{3,2,4,1,0:T(8,128)S(1)} %get-tuple-element.224) | copy-start | bytes 25165828 | tf_op jit(solution)/shard_map/while
  173.9 5.2 %copy-start.6 = (f32[2,4,8,128,128]{4,3,2,1,0:T(8,128)S(1)}, f32[2,4,8,128,128]{4,3,2,1,0:T(8,128)}, u32[]{:S(2)}) copy-start(f32[2,4,8,128,128]{4,3,2,1,0:T(8,128)} %get-tuple-element.244) | copy-start | bytes 12582916 | tf_op jit(solution)/shard_map/while
  182.3 2.0 copy-start.7
  185.1 7.8 %copy-start.3 = (f32[4,8,128,128,4]{3,2,4,1,0:T(8,128)S(1)}, f32[4,8,128,128,4]{3,2,4,1,0:T(8,128)}, u32[]{:S(2)}) copy-start(f32[4,8,128,128,4]{3,2,4,1,0:T(8,128)} %copy-done.2) | copy-start | bytes 25165828 | tf_op jit(solution)/shard_map/while
  192.8 4.4 copy-start.4
  197.2 4.4 copy-start.10
  198.5 1.9 copy-start.5
  201.8 1.0 copy-start.11
  206.5 8.4 %copy-start.2 = (f32[4,8,128,128,4]{3,2,4,1,0:T(8,128)}, f32[4,8,128,128,4]{3,2,4,1,0:T(8,128)S(1)}, u32[]{:S(2)}) copy-start(f32[4,8,128,128,4]{3,2,4,1,0:T(8,128)S(1)} %get-tuple-element.224) | copy-start | bytes 25165828 | tf_op jit(solution)/shard_map/while
  206.5 5.2 %copy-start.6 = (f32[2,4,8,128,128]{4,3,2,1,0:T(8,128)S(1)}, f32[2,4,8,128,128]{4,3,2,1,0:T(8,128)}, u32[]{:S(2)}) copy-start(f32[2,4,8,128,128]{4,3,2,1,0:T(8,128)} %get-tuple-element.244) | copy-start | bytes 12582916 | tf_op jit(solution)/shard_map/while
  215.0 2.0 copy-start.7
  217.7 7.8 %copy-start.3 = (f32[4,8,128,128,4]{3,2,4,1,0:T(8,128)S(1)}, f32[4,8,128,128,4]{3,2,4,1,0:T(8,128)}, u32[]{:S(2)}) copy-start(f32[4,8,128,128,4]{3,2,4,1,0:T(8,128)} %copy-done.2) | copy-start | bytes 25165828 | tf_op jit(solution)/shard_map/while
  225.5 4.4 copy-start.4
  229.9 4.4 copy-start.10
  231.1 1.9 copy-start.5
  234.4 1.0 copy-start.11
  235.4 7.4 %copy-start.8 = (f32[2,4,8,128,128]{4,3,2,1,0:T(8,128)S(1)}, f32[2,4,8,128,128]{4,3,2,1,0:T(8,128)}, u32[]{:S(2)}) copy-start(f32[2,4,8,128,128]{4,3,2,1,0:T(8,128)} %get-tuple-element.66) | copy-start | bytes 12582916
  248.0 2.9 collective-permute-start.4
  248.3 8.8 %copy-start.12 = (bf16[2,4,128,4,128]{4,3,2,1,0:T(4,128)(2,1)S(1)}, bf16[2,4,128,4,128]{4,3,2,1,0:T(4,128)(2,1)}, u32[]{:S(2)}) copy-start(bf16[2,4,128,4,128]{4,3,2,1,0:T(4,128)(2,1)} %get-tuple-element.64) | copy-start | bytes 3145732
  257.0 190.2 %reduce-scatter.3.cloned.1.call-start = ((), (), s32[]{:S(2)}) async-start(), calls=%async_computation.5 | async-start | bytes 10485760 | tf_op jit(solution)/shard_map/reduce_scatter | solution.py:142
  267.5 1.2 copy-start.13
  268.7 181.4 %copy-start.1 = (s32[4,8,8]{2,1,0:T(8,128)S(1)}, s32[4,8,8]{2,1,0:T(8,128)}, u32[]{:S(2)}) copy-start(s32[4,8,8]{2,1,0:T(8,128)} %param.12) | copy-start | bytes 3076
Sparse Core Ops, SparseCore 0:
  9.6 90.1 all-gather.3
  101.6 53.5 all-gather.5
  257.2 43.7 reduce-scatter.4
  303.3 143.8 reduce-scatter.2
